TPU v7x, 32 devices: a whole 2x2x4 slice. The times are simulated.
32 devices in a mesh: rep: 4 (over y, core), shard: 8 (over z, x).
Axes of the slice: x: 2, y: 2, z: 4, core: 2. Of those that a mesh axis runs over, the one named last changes fastest.
Arguments:
- cell_features: bfloat16 [4, 4096, 1024], P('rep', 'shard'), may hold values from -10 to 10
- upstream: bfloat16 [4, 4096, 1024], P('rep', 'shard'), may hold values from -0.119628906 to 0.119628906
- qkv_weight: bfloat16 [4, 1024, 3072], P('rep', 'shard'), may hold values from -0.1875 to 0.1875
- out_weight: bfloat16 [4, 1024, 1024], P('rep', 'shard'), may hold values from -0.1875 to 0.1875
- momentum: float32 [4, 1024, 1024], P('rep', 'shard'), may hold values from -4 to 4
- key_tiles: int32 [4, 32, 6], P('rep'), may hold values from 0 to 31, as said below
- live_blocks: int32 [4, 32], P('rep'), may hold values from 1 to 6
- step_index: int32 [], replicated, may hold values from 0 to 999
Outputs:
- layer_out: bfloat16 [4, 4096, 1024], P('rep', 'shard')
- new_weight: bfloat16 [4, 1024, 1024], P('rep', 'shard')
- new_momentum: float32 [4, 1024, 1024], P('rep', 'shard')
Inputs may be any that keep to these rules, and one draw needn't show every extreme that they name: `key_tiles`: every entry names a tile of its group. Of the 24 entries of device d's 4 query tiles (tiles d*4 to (d+1)*4 - 1), exactly 12 name tiles of device d itself (tile // 4 == d); of the others at most 2 name tiles of any one other device, and in every draw some device is named exactly 2 times.
All inputs are finite; a program needn't handle non-finite values.
Results may differ from a plain program's by a relative error of at most 0.025.
Values may be sent and summed in bfloat16 or wider, within the bound.
No kernel may reach another device: no remote copies, remote signals or barrier semaphores. Data moves between devices by JAX's collectives and lax.ppermute only.
A program may use at most 128 MiB of HBM per device.

v0:
```python
import functools
import jax
import jax.numpy as jnp
from jax import lax
from jax.sharding import PartitionSpec as P

HEADS = 16
HEAD_DIM = 64
TILE = 128
KB = 6
momentum_beta = 0.9


def shortened(value):

    def short(part):
        return part.astype(jnp.bfloat16) if part.dtype == jnp.float32 else part

    return jax.tree.map(short, value)


def partner(value, axis, bit):
    return lax.ppermute(value, axis, [(i, i ^ 1 << bit) for i in range(lax.axis_size(axis))])


def add_rows(source, shard_rows):
    return jnp.dot(source, shard_rows, preferred_element_type=jnp.float32)


def attend_tile(local_table, arrived_table, element):
    query_tile, is_remote, local_index, arrive_index, live_count = element
    model_width = query_tile.shape[1]
    from_local = local_table[local_index]
    from_remote = arrived_table[arrive_index]
    key_value = jnp.where(is_remote[:, None, None], from_remote, from_local).reshape(
        KB * TILE, 2 * model_width
    )
    query_split = query_tile.reshape(TILE, HEADS, HEAD_DIM)
    keys_split = key_value[:, :model_width].reshape(KB * TILE, HEADS, HEAD_DIM)
    values_split = key_value[:, model_width:].reshape(KB * TILE, HEADS, HEAD_DIM)
    scores = jnp.einsum(
        "qhd,khd->hqk", query_split, keys_split, preferred_element_type=jnp.float32
    ) * HEAD_DIM ** (-0.5)
    usable = jnp.arange(KB * TILE, dtype=jnp.int32) // TILE < live_count
    scores = jnp.where(usable[None, None, :], scores, jnp.float32(-1e30))
    row_max = jnp.max(scores, axis=2, keepdims=True)
    exponent = jnp.exp(scores - row_max)
    probabilities = (exponent / jnp.sum(exponent, axis=2, keepdims=True)).astype(jnp.bfloat16)
    mixture = jnp.einsum(
        "hqk,khd->qhd", probabilities, values_split, preferred_element_type=jnp.float32
    )
    return mixture.reshape(TILE, model_width).astype(jnp.bfloat16)


def swap_with(bit_number, stacked_pair):
    return jax.tree.map(
        lambda part, own: part.astype(own.dtype),
        partner(shortened(stacked_pair), "rep", bit_number),
        stacked_pair,
    )


def body(
    cell_features, upstream, qkv_weight, out_weight, momentum, key_tiles, live_blocks, step_index
):
    features = cell_features[0]
    row_count, model_width = features.shape
    tile_count = row_count // TILE
    shard_count = lax.axis_size("shard")
    my_index = lax.axis_index("shard")
    slot_count = tile_count * KB
    remote_count = slot_count - slot_count // 2
    capacity = (remote_count + shard_count - 2) // (shard_count - 1)
    requests = key_tiles[0].reshape(shard_count, slot_count)
    owners = requests // tile_count
    local_tile = requests % tile_count
    requester = jnp.arange(shard_count, dtype=jnp.int32)[:, None]
    elsewhere = owners != requester
    positions = jnp.arange(slot_count, dtype=jnp.int32)
    earlier = positions[None, :] < positions[:, None]
    same_owner = owners[:, :, None] == owners[:, None, :]
    owner_rank = jnp.sum((same_owner & earlier[None]).astype(jnp.int32), axis=2)
    owned = (owners == my_index) & elsewhere
    slot_ids = jnp.arange(capacity, dtype=jnp.int32)
    chosen = owned[:, :, None] & (owner_rank[:, :, None] == slot_ids[None, None, :])
    send_index = jnp.sum(chosen.astype(jnp.int32) * local_tile[:, :, None], axis=1).reshape(-1)
    send_valid = jnp.any(chosen, axis=1).reshape(-1)
    my_owners = lax.dynamic_index_in_dim(owners, my_index, 0, keepdims=False)
    my_ranks = lax.dynamic_index_in_dim(owner_rank, my_index, 0, keepdims=False)
    my_local = lax.dynamic_index_in_dim(local_tile, my_index, 0, keepdims=False)
    my_remote = my_owners != my_index
    arrive_index = jnp.where(my_remote, my_owners * capacity + my_ranks, 0)
    local_index = jnp.where(my_remote, 0, my_local)
    projected = add_rows(
        features, lax.all_gather(qkv_weight[0], "shard", axis=0, tiled=True)
    ).astype(jnp.bfloat16)
    picked = projected[:, model_width:].reshape(tile_count, TILE, 2 * model_width)[send_index]
    sent = jnp.where(send_valid[:, None, None], picked, jnp.zeros_like(picked)).reshape(
        shard_count, capacity, TILE, 2 * model_width
    )
    arrived = lax.all_to_all(sent, "shard", split_axis=0, concat_axis=0, tiled=True)
    arrived_table = arrived.reshape(shard_count * capacity, TILE, 2 * model_width)
    query = projected[:, :model_width].reshape(tile_count, TILE, model_width)
    local_table = projected[:, model_width:].reshape(tile_count, TILE, 2 * model_width)
    live_mine = lax.dynamic_slice_in_dim(live_blocks[0], my_index * tile_count, tile_count, 0)
    per_tile = functools.partial(attend_tile, local_table, arrived_table)
    elements = (
        query,
        my_remote.reshape(tile_count, KB),
        local_index.reshape(tile_count, KB),
        arrive_index.reshape(tile_count, KB),
        live_mine,
    )
    attended = lax.map(per_tile, elements).reshape(row_count, model_width)
    product = add_rows(attended, lax.all_gather(out_weight[0], "shard", axis=0, tiled=True))
    layer_out = (features.astype(jnp.float32) + product).astype(jnp.bfloat16)
    gradient = lax.psum_scatter(
        lax.dot_general(
            attended, upstream[0], (((0,), (0,)), ((), ())), preferred_element_type=jnp.float32
        ).astype(jnp.bfloat16),
        "shard",
        scatter_dimension=0,
        tiled=True,
    ).astype(jnp.float32)
    learn_rate = jnp.float32(50.0) / (jnp.float32(500.0) + step_index.astype(jnp.float32))
    velocity = momentum_beta * momentum[0] + gradient
    stepped = (out_weight[0].astype(jnp.float32) - learn_rate * velocity).astype(jnp.bfloat16)
    stacked_pair = jnp.stack([stepped.astype(jnp.float32), velocity])
    bit_count = lax.axis_size("rep").bit_length() - 1
    branches = [functools.partial(swap_with, bit_number) for bit_number in range(bit_count)]
    bit_choice = step_index % bit_count
    partner_pair = lax.switch(bit_choice, branches, stacked_pair)
    averaged = 0.5 * (stacked_pair + partner_pair)
    new_weight = averaged[0].astype(jnp.bfloat16)
    new_momentum = averaged[1]
    return (layer_out[None], new_weight[None], new_momentum[None])


def solution(mesh):
    placed = (
        P("rep", "shard", None),
        P("rep", "shard", None),
        P("rep", "shard", None),
        P("rep", "shard", None),
        P("rep", "shard", None),
        P("rep", None, None),
        P("rep", None),
        P(),
    )
    return jax.shard_map(
        body,
        mesh=mesh,
        in_specs=placed,
        out_specs=(P("rep", "shard", None), P("rep", "shard", None), P("rep", "shard", None)),
        check_vma=False,
    )
```

profile of v0, /device:TPU:0, one launch (start us, length us, event | category | flops | bytes accessed | tf_op | source)
XLA Modules:
  0.0 585.2 jit_solution(10328500597849223528)
XLA Ops:
  9.7 101.9 %all-gather.5.cloned.1.call-done = bf16[1,1024,3072]{2,1,0:T(8,128)(2,1)} async-done(((bf16[1,128,3072]{2,1,0:T(8,128)(2,1)}), bf16[1,1024,3072]{2,1,0:T(8,128)(2,1)}) %all-gather.5.cloned.1.call-update) | async-done | bytes 6291472 | tf_op jit(solution)/shard_map/all_gather | solution.py:95
  111.6 6.5 %fusion.21 = bf16[512,3072]{1,0:T(8,128)(2,1)S(1)} fusion(bf16[1,1024,3072]{2,1,0:T(8,128)(2,1)} %all-gather.5.cloned.1.call-done, bf16[1,512,1024]{2,1,0:T(8,128)(2,1)} %param.12), kind=kOutput, calls=%fused_computation.42 | convolution fusion | flops 3222798336 | bytes 10485760 | tf_op jit(solution)/shard_map/dot_general | solution.py:27
  124.7 7.2 %broadcast_select_fusion.1 = bf16[8,2,128,2048]{3,2,1,0:T(8,128)(2,1)} fusion(bf16[8,2,128,2048]{3,2,1,0:T(8,128)(2,1)} %bitcast.120, pred[8,2]{1,0:T(8,128)(4,1)S(1)} %copy.22), kind=kLoop, calls=%fused_computation.39 | loop fusion | flops 4194304 | bytes 16777232 | tf_op jit(solution)/shard_map/jit(_where)/select_n | solution.py:98
  131.9 5.1 all-to-all-start
  140.6 203.7 %all-to-all-done = bf16[8,2,128,2048]{3,2,1,0:T(8,128)(2,1)} async-done(((bf16[8,2,128,2048]{3,2,1,0:T(8,128)(2,1)}), bf16[8,2,128,2048]{3,2,1,0:T(8,128)(2,1)}, u32[]{:S(2)}, u32[]{:S(2)}) %all-to-all-start) | async-done | bytes 8388640 | tf_op jit(solution)/shard_map/all_to_all | solution.py:101
  344.3 157.9 %while.12 = (s32[]{:T(128)}, bf16[4,128,1024]{2,1,0:T(8,128)(2,1)}, pred[4,6]{1,0:T(4,128)(4,1)S(1)}, s32[4,6]{1,0:T(4,128)S(1)}, bf16[16,128,2048]{2,1,0:T(8,12...) while((s32[]{:T(128)}, bf16[4,128,1024]{2,1,0:T(8,128)(2,1)}, ...), condition=%wide.region_6.7_spmd, body=%wide.region_3.6_spmd.sunk | while | flops 413804064 | bytes 59273044 | solution.py:114
  344.3 6.0 %gather_fusion = bf16[6,128,2048]{2,1,0:T(8,128)(2,1)} fusion(bf16[16,128,2048]{2,1,0:T(8,128)(2,1)} %get-tuple-element.279, s32[1024]{0:T(1024)S(1)} %pad_clamp_fusion.5), kind=kCustom, calls=%fused_computation.clone.1 | custom fusion | bytes 6291480 | tf_op jit(solution)/shard_map/while/body/eval_jaxpr/gather | solution.py:34
  350.3 4.7 copy.33
  357.4 4.6 copy.34
  370.3 6.4 %fusion.70 = (f32[16,128]{1,0:T(8,128)S(1)}, f32[16,128,768]{2,1,0:T(8,128)}) fusion(pred[768]{0:T(1024)(128)(4,1)S(1)} %fusion.69, bf16[128,16,64]{0,2,1:T(8,128)(2,1)} %bitcast.121, bf16[768,16,64]{0,2,1:T(8,128)(2,1)} %bitcast.119), kind=kOutput, calls=%fused_computation.90.clone.1 | convolution fusion | flops 207618816 | bytes 8135424 | tf_op jit(solution)/shard_map/while/body/eval_jaxpr/sub | solution.py:47
  376.7 5.3 fusion.71
  383.8 6.0 %gather_fusion = bf16[6,128,2048]{2,1,0:T(8,128)(2,1)} fusion(bf16[16,128,2048]{2,1,0:T(8,128)(2,1)} %get-tuple-element.279, s32[1024]{0:T(1024)S(1)} %pad_clamp_fusion.5), kind=kCustom, calls=%fused_computation.clone.1 | custom fusion | bytes 6291480 | tf_op jit(solution)/shard_map/while/body/eval_jaxpr/gather | solution.py:34
  389.8 4.7 copy.33
  409.7 6.4 %fusion.70 = (f32[16,128]{1,0:T(8,128)S(1)}, f32[16,128,768]{2,1,0:T(8,128)}) fusion(pred[768]{0:T(1024)(128)(4,1)S(1)} %fusion.69, bf16[128,16,64]{0,2,1:T(8,128)(2,1)} %bitcast.121, bf16[768,16,64]{0,2,1:T(8,128)(2,1)} %bitcast.119), kind=kOutput, calls=%fused_computation.90.clone.1 | convolution fusion | flops 207618816 | bytes 8135424 | tf_op jit(solution)/shard_map/while/body/eval_jaxpr/sub | solution.py:47
  416.1 5.3 fusion.71
  423.3 6.0 %gather_fusion = bf16[6,128,2048]{2,1,0:T(8,128)(2,1)} fusion(bf16[16,128,2048]{2,1,0:T(8,128)(2,1)} %get-tuple-element.279, s32[1024]{0:T(1024)S(1)} %pad_clamp_fusion.5), kind=kCustom, calls=%fused_computation.clone.1 | custom fusion | bytes 6291480 | tf_op jit(solution)/shard_map/while/body/eval_jaxpr/gather | solution.py:34
  429.2 4.7 copy.33
  449.2 6.4 %fusion.70 = (f32[16,128]{1,0:T(8,128)S(1)}, f32[16,128,768]{2,1,0:T(8,128)}) fusion(pred[768]{0:T(1024)(128)(4,1)S(1)} %fusion.69, bf16[128,16,64]{0,2,1:T(8,128)(2,1)} %bitcast.121, bf16[768,16,64]{0,2,1:T(8,128)(2,1)} %bitcast.119), kind=kOutput, calls=%fused_computation.90.clone.1 | convolution fusion | flops 207618816 | bytes 8135424 | tf_op jit(solution)/shard_map/while/body/eval_jaxpr/sub | solution.py:47
  455.6 5.3 fusion.71
  462.8 6.0 %gather_fusion = bf16[6,128,2048]{2,1,0:T(8,128)(2,1)} fusion(bf16[16,128,2048]{2,1,0:T(8,128)(2,1)} %get-tuple-element.279, s32[1024]{0:T(1024)S(1)} %pad_clamp_fusion.5), kind=kCustom, calls=%fused_computation.clone.1 | custom fusion | bytes 6291480 | tf_op jit(solution)/shard_map/while/body/eval_jaxpr/gather | solution.py:34
  468.7 4.7 copy.33
  488.7 6.4 %fusion.70 = (f32[16,128]{1,0:T(8,128)S(1)}, f32[16,128,768]{2,1,0:T(8,128)}) fusion(pred[768]{0:T(1024)(128)(4,1)S(1)} %fusion.69, bf16[128,16,64]{0,2,1:T(8,128)(2,1)} %bitcast.121, bf16[768,16,64]{0,2,1:T(8,128)(2,1)} %bitcast.119), kind=kOutput, calls=%fused_computation.90.clone.1 | convolution fusion | flops 207618816 | bytes 8135424 | tf_op jit(solution)/shard_map/while/body/eval_jaxpr/sub | solution.py:47
  495.1 5.3 fusion.71
  511.1 62.4 %reduce-scatter.2.cloned.1.call-done = bf16[128,1024]{1,0:T(8,128)(2,1)} async-done(((bf16[1024,1024]{1,0:T(8,128)(2,1)}), bf16[128,1024]{1,0:T(8,128)(2,1)}) %reduce-scatter.2.cloned.1.call-update) | async-done | bytes 262160 | tf_op jit(solution)/shard_map/reduce_scatter | solution.py:117
  (113 shorter events, 91.7 us)
Async XLA Ops:
  7.2 495.0 %copy-start = (bf16[1,512,1024]{2,1,0:T(8,128)(2,1)S(1)}, bf16[1,512,1024]{2,1,0:T(8,128)(2,1)}, u32[]{:S(2)}) copy-start(bf16[1,512,1024]{2,1,0:T(8,128)(2,1)} %param.13) | copy-start | bytes 3145732
  7.2 104.4 %all-gather.5.cloned.1.call-start = ((), (), s32[]{:S(2)}) async-start(), calls=%async_computation.3 | async-start | bytes 7077888 | tf_op jit(solution)/shard_map/all_gather | solution.py:95
  118.2 1.7 copy-start.1
  131.9 6.4 %copy-start.5 = (s32[1,32]{1,0:T(1,128)S(1)}, s32[1,32]{1,0:T(1,128)}, u32[]{:S(2)}) copy-start(s32[1,32]{1,0:T(1,128)} %param.18) | copy-start | bytes 388
  131.9 212.4 %all-to-all-start = ((bf16[8,2,128,2048]{3,2,1,0:T(8,128)(2,1)}), bf16[8,2,128,2048]{3,2,1,0:T(8,128)(2,1)}, u32[]{:S(2)}, u32[]{:S(2)}) async-start(bf16[8,2,128,2048]{3,2,1,0:T(8,128)(2,1)} %broadcast_select_fusion.1), calls=%async_computation | async-start | bytes 16777216 | tf_op jit(solution)/shard_map/all_to_all | solution.py:101
  136.9 370.0 %all-gather.7.cloned.1.call-start = ((), (), s32[]{:S(2)}) async-start(), calls=%async_computation.4 | async-start | bytes 2359296 | tf_op jit(solution)/shard_map/all_gather | solution.py:115
  137.7 435.9 %reduce-scatter.2.cloned.1.call-start = ((), (), s32[]{:S(2)}) async-start(), calls=%async_computation.2 | async-start | bytes 2359296 | tf_op jit(solution)/shard_map/reduce_scatter | solution.py:117
  502.2 4.7 copy-start.4
  506.9 66.7 %copy-start.2 = (bf16[1,128,1024]{2,1,0:T(8,128)(2,1)S(1)}, bf16[1,128,1024]{2,1,0:T(8,128)(2,1)}, u32[]{:S(2)}) copy-start(bf16[1,128,1024]{2,1,0:T(8,128)(2,1)} %param.15) | copy-start | bytes 786436
  506.9 66.7 %copy-start.3 = (f32[1,128,1024]{2,1,0:T(8,128)S(1)}, f32[1,128,1024]{2,1,0:T(8,128)}, u32[]{:S(2)}) copy-start(f32[1,128,1024]{2,1,0:T(8,128)} %param.16) | copy-start | bytes 1572868
  574.8 2.0 collective-permute-start
Sparse Core Ops, SparseCore 0:
  10.2 101.3 all-gather.4
  139.9 169.2 all-gather.6
  506.3 67.2 reduce-scatter.1
where the time goes:
time: 587 us; the launch traced here: 585 us
  waiting for transfers between devices  371 us (63%)
  local copies, waits for them, and re-layouts  108 us (18%)
  matrix products  61.4 us (10%)
  other arithmetic  24.6 us (4%)
  between operations  14.6 us (2%)
    all_to_all x1, waiting for transfers between devices, body(): lax.all_to_all(sent, 'shard', split_axis=0, concat_axis=0, tiled=True)  204 us
    all_gather x1, waiting for transfers between devices, body(): lax.all_gather(qkv_weight[0], 'shard', axis=0, tiled=True)  102 us
    reduce_scatter x1, waiting for transfers between devices, body(): lax.psum_scatter(lax.dot_general(attended, upstream[0], (((0,), (0,)), ((...  62.4 us
    gather x8, local copies, waits for them, and re-layouts, attend_tile(): from_remote = arrived_table[arrive_index]  42.6 us
    gather x8, local copies, waits for them, and re-layouts, attend_tile(): from_local = local_table[local_index]  28.5 us
    sub x4, matrix products, attend_tile(): exponent = jnp.exp(scores - row_max)  25.6 us
    dot_general x4, matrix products, attend_tile(): jnp.einsum('hqk,khd->qhd', probabilities, values_split, preferred_element...  21.1 us
    select_n x4, other arithmetic, attend_tile(): jnp.where(is_remote[:, None, None], from_remote, from_local)  12.7 us
  transfers between devices with their start and end apart: 5, of which 4 were waited for; matrix products, arithmetic and copies ran while one was open for 29% of the time, Pallas kernels for 0%

commit v1 on v0

--- a/solution.py
+++ b/solution.py
@@ -9,6 +9,22 @@
 TILE = 128
 KB = 6
 momentum_beta = 0.9
+
+
+def collect(x, axis, dim):
+    ways, here, step = (lax.axis_size(axis), lax.axis_index(axis), x.shape[dim])
+    dims = [n * ways if d == dim else n for d, n in enumerate(x.shape)]
+    full = lax.dynamic_update_slice_in_dim(jnp.zeros(dims, x.dtype), x, here * step, axis=dim)
+    going_up = going_down = x
+    for far in range(1, ways // 2 + 1):
+        going_up = lax.ppermute(going_up, axis, [(d, (d + 1) % ways) for d in range(ways)])
+        full = lax.dynamic_update_slice_in_dim(full, going_up, (here - far) % ways * step, axis=dim)
+        if 2 * far < ways:
+            going_down = lax.ppermute(going_down, axis, [(d, (d - 1) % ways) for d in range(ways)])
+            full = lax.dynamic_update_slice_in_dim(
+                full, going_down, (here + far) % ways * step, axis=dim
+            )
+    return full
 
 
 def shortened(value):
@@ -91,9 +107,7 @@
     my_remote = my_owners != my_index
     arrive_index = jnp.where(my_remote, my_owners * capacity + my_ranks, 0)
     local_index = jnp.where(my_remote, 0, my_local)
-    projected = add_rows(
-        features, lax.all_gather(qkv_weight[0], "shard", axis=0, tiled=True)
-    ).astype(jnp.bfloat16)
+    projected = add_rows(features, collect(qkv_weight[0], "shard", 0)).astype(jnp.bfloat16)
     picked = projected[:, model_width:].reshape(tile_count, TILE, 2 * model_width)[send_index]
     sent = jnp.where(send_valid[:, None, None], picked, jnp.zeros_like(picked)).reshape(
         shard_count, capacity, TILE, 2 * model_width

time: 587 us -> 605 us (1.031)
  starting transfers between devices: 5.45 us -> 24.5 us
    ppermute x0 -> x7, waiting for transfers between devices: none -> 105 us  [the longest x4 86.5 us: collect(): lax.ppermute(going_up, axis, [(d, (d + 1) % ways) for d in range(ways)])]
    all_gather x1 -> x0, waiting for transfers between devices: 102 us -> none  [body(): lax.all_gather(qkv_weight[0], 'shard', axis=0, tiled=True)]
    ppermute x0 -> x7, starting transfers between devices: none -> 19.1 us  [the longest x4 10.4 us: collect(): lax.ppermute(going_up, axis, [(d, (d + 1) % ways) for d in range(ways)])]
  transfers between devices with their start and end apart: 5 -> 11, of which waited for: 4 -> 8; matrix products, arithmetic and copies ran while one was open for 29% -> 28% of each run, Pallas kernels for 0% -> 0%
where the time goes in v1:
time: 605 us; the launch traced here: 603 us
  waiting for transfers between devices  372 us (61%)
  local copies, waits for them, and re-layouts  109 us (18%)
  matrix products  58.4 us (10%)
  other arithmetic  24.7 us (4%)
  starting transfers between devices  24.5 us (4%)
  between operations  15.1 us (2%)
    all_to_all x1, waiting for transfers between devices, body(): lax.all_to_all(sent, 'shard', split_axis=0, concat_axis=0, tiled=True)  202 us
    ppermute x4, waiting for transfers between devices, collect(): lax.ppermute(going_up, axis, [(d, (d + 1) % ways) for d in range(ways)])  86.5 us
    reduce_scatter x1, waiting for transfers between devices, body(): lax.psum_scatter(lax.dot_general(attended, upstream[0], (((0,), (0,)), ((...  62.4 us
    gather x8, local copies, waits for them, and re-layouts, attend_tile(): from_remote = arrived_table[arrive_index]  42.7 us
    gather x8, local copies, waits for them, and re-layouts, attend_tile(): from_local = local_table[local_index]  28.5 us
    sub x4, matrix products, attend_tile(): exponent = jnp.exp(scores - row_max)  25.6 us
    dot_general x4, matrix products, attend_tile(): jnp.einsum('hqk,khd->qhd', probabilities, values_split, preferred_element...  21.1 us
    ppermute x3, waiting for transfers between devices, collect(): lax.ppermute(going_down, axis, [(d, (d - 1) % ways) for d in range(ways)])  18.5 us
  transfers between devices with their start and end apart: 11, of which 8 were waited for; matrix products, arithmetic and copies ran while one was open for 28% of the time, Pallas kernels for 0%

profile of v1, /device:TPU:0, one launch (start us, length us, event | category | flops | bytes accessed | tf_op | source)
XLA Modules:
  0.0 603.3 jit_solution(4436289065777069354)
XLA Ops:
  15.1 29.1 %collective-permute-done.2 = bf16[128,3072]{1,0:T(8,128)(2,1)S(1)} collective-permute-done((bf16[128,3072]{1,0:T(8,128)(2,1)}, bf16[128,3072]{1,0:T(8,128)(2,1)S(1)}, u32[]{:S(2)}, u32[]{:S(2)}) %collective-permute-start.2) | collective-permute-done | bytes 786464 | tf_op jit(solution)/shard_map/ppermute | solution.py:20
  50.5 28.8 %collective-permute-done.4 = bf16[128,3072]{1,0:T(8,128)(2,1)S(1)} collective-permute-done((bf16[128,3072]{1,0:T(8,128)(2,1)S(1)}, bf16[128,3072]{1,0:T(8,128)(2,1)S(1)}, u32[]{:S(2)}, u32[]{:S(2)}) %collective-permute-start.4) | collective-permute-done | bytes 786464 | tf_op jit(solution)/shard_map/ppermute | solution.py:20
  85.2 28.6 %collective-permute-done.6 = bf16[128,3072]{1,0:T(8,128)(2,1)S(1)} collective-permute-done((bf16[128,3072]{1,0:T(8,128)(2,1)S(1)}, bf16[128,3072]{1,0:T(8,128)(2,1)S(1)}, u32[]{:S(2)}, u32[]{:S(2)}) %collective-permute-start.6) | collective-permute-done | bytes 786464 | tf_op jit(solution)/shard_map/ppermute | solution.py:20
  116.4 18.0 %collective-permute-done.7 = bf16[128,3072]{1,0:T(8,128)(2,1)S(1)} collective-permute-done((bf16[128,3072]{1,0:T(8,128)(2,1)S(1)}, bf16[128,3072]{1,0:T(8,128)(2,1)S(1)}, u32[]{:S(2)}, u32[]{:S(2)}) %collective-permute-start.7) | collective-permute-done | bytes 786464 | tf_op jit(solution)/shard_map/ppermute | solution.py:23
  144.8 7.2 %broadcast_select_fusion.1 = bf16[8,2,128,2048]{3,2,1,0:T(8,128)(2,1)} fusion(bf16[8,2,128,2048]{3,2,1,0:T(8,128)(2,1)} %bitcast.120, pred[8,2]{1,0:T(8,128)(4,1)S(1)} %copy.22), kind=kLoop, calls=%fused_computation.39 | loop fusion | flops 4194304 | bytes 16777232 | tf_op jit(solution)/shard_map/jit(_where)/select_n | solution.py:112
  152.0 5.1 all-to-all-start
  160.7 201.5 %all-to-all-done = bf16[8,2,128,2048]{3,2,1,0:T(8,128)(2,1)} async-done(((bf16[8,2,128,2048]{3,2,1,0:T(8,128)(2,1)}), bf16[8,2,128,2048]{3,2,1,0:T(8,128)(2,1)}, u32[]{:S(2)}, u32[]{:S(2)}) %all-to-all-start) | async-done | bytes 8388640 | tf_op jit(solution)/shard_map/all_to_all | solution.py:115
  362.2 157.8 %while.12 = (s32[]{:T(128)}, bf16[4,128,1024]{2,1,0:T(8,128)(2,1)}, pred[4,6]{1,0:T(4,128)(4,1)S(1)}, s32[4,6]{1,0:T(4,128)S(1)}, bf16[16,128,2048]{2,1,0:T(8,12...) while((s32[]{:T(128)}, bf16[4,128,1024]{2,1,0:T(8,128)(2,1)}, ...), condition=%wide.region_6.7_spmd, body=%wide.region_3.6_spmd.sunk | while | flops 413804064 | bytes 59273044 | solution.py:128
  362.2 6.0 gather_fusion
  368.2 4.7 copy.33
  388.2 6.4 %fusion.67 = (f32[16,128]{1,0:T(8,128)S(1)}, f32[16,128,768]{2,1,0:T(8,128)}) fusion(pred[768]{0:T(1024)(128)(4,1)S(1)} %fusion.66, bf16[128,16,64]{0,2,1:T(8,128)(2,1)} %bitcast.121, bf16[768,16,64]{0,2,1:T(8,128)(2,1)} %bitcast.119), kind=kOutput, calls=%fused_computation.97.clone.1 | convolution fusion | flops 207618816 | bytes 8135424 | tf_op jit(solution)/shard_map/while/body/eval_jaxpr/sub | solution.py:63
  394.6 5.3 fusion.68
  401.7 6.0 gather_fusion
  407.7 4.7 copy.33
  427.6 6.4 %fusion.67 = (f32[16,128]{1,0:T(8,128)S(1)}, f32[16,128,768]{2,1,0:T(8,128)}) fusion(pred[768]{0:T(1024)(128)(4,1)S(1)} %fusion.66, bf16[128,16,64]{0,2,1:T(8,128)(2,1)} %bitcast.121, bf16[768,16,64]{0,2,1:T(8,128)(2,1)} %bitcast.119), kind=kOutput, calls=%fused_computation.97.clone.1 | convolution fusion | flops 207618816 | bytes 8135424 | tf_op jit(solution)/shard_map/while/body/eval_jaxpr/sub | solution.py:63
  434.0 5.3 fusion.68
  441.1 6.0 gather_fusion
  447.1 4.7 copy.33
  467.1 6.4 %fusion.67 = (f32[16,128]{1,0:T(8,128)S(1)}, f32[16,128,768]{2,1,0:T(8,128)}) fusion(pred[768]{0:T(1024)(128)(4,1)S(1)} %fusion.66, bf16[128,16,64]{0,2,1:T(8,128)(2,1)} %bitcast.121, bf16[768,16,64]{0,2,1:T(8,128)(2,1)} %bitcast.119), kind=kOutput, calls=%fused_computation.97.clone.1 | convolution fusion | flops 207618816 | bytes 8135424 | tf_op jit(solution)/shard_map/while/body/eval_jaxpr/sub | solution.py:63
  473.5 5.3 fusion.68
  480.6 6.0 gather_fusion
  506.5 6.4 %fusion.67 = (f32[16,128]{1,0:T(8,128)S(1)}, f32[16,128,768]{2,1,0:T(8,128)}) fusion(pred[768]{0:T(1024)(128)(4,1)S(1)} %fusion.66, bf16[128,16,64]{0,2,1:T(8,128)(2,1)} %bitcast.121, bf16[768,16,64]{0,2,1:T(8,128)(2,1)} %bitcast.119), kind=kOutput, calls=%fused_computation.97.clone.1 | convolution fusion | flops 207618816 | bytes 8135424 | tf_op jit(solution)/shard_map/while/body/eval_jaxpr/sub | solution.py:63
  512.9 5.3 fusion.68
  529.0 62.4 %reduce-scatter.2.cloned.1.call-done = bf16[128,1024]{1,0:T(8,128)(2,1)} async-done(((bf16[1024,1024]{1,0:T(8,128)(2,1)}), bf16[128,1024]{1,0:T(8,128)(2,1)}) %reduce-scatter.2.cloned.1.call-update) | async-done | bytes 262160 | tf_op jit(solution)/shard_map/reduce_scatter | solution.py:131
  (137 shorter events, 124.8 us)
Async XLA Ops:
  7.2 512.8 %copy-start = (bf16[1,512,1024]{2,1,0:T(8,128)(2,1)S(1)}, bf16[1,512,1024]{2,1,0:T(8,128)(2,1)}, u32[]{:S(2)}) copy-start(bf16[1,512,1024]{2,1,0:T(8,128)(2,1)} %param.13) | copy-start | bytes 3145732
  7.2 40.2 %copy-start.3 = (bf16[1,128,3072]{2,1,0:T(8,128)(2,1)S(1)}, bf16[1,128,3072]{2,1,0:T(8,128)(2,1)}, u32[]{:S(2)}) copy-start(bf16[1,128,3072]{2,1,0:T(8,128)(2,1)} %param.14) | copy-start | bytes 2359300
  7.2 37.0 %collective-permute-start.2 = (bf16[128,3072]{1,0:T(8,128)(2,1)}, bf16[128,3072]{1,0:T(8,128)(2,1)S(1)}, u32[]{:S(2)}, u32[]{:S(2)}) collective-permute-start(bf16[128,3072]{1,0:T(8,128)(2,1)} %bitcast.124), channel_id=1, source_target_pairs={{0,1},{1,2},{2,3},{3,4},{4,5},{5,6},{6,7},{7,0},{8,9},{9,10},{10,1... | collective-permute-start | bytes 2359304 | tf_op jit(solution)/shard_map/ppermute | solution.py:20
  10.2 37.2 %collective-permute-start.3 = (bf16[128,3072]{1,0:T(8,128)(2,1)}, bf16[128,3072]{1,0:T(8,128)(2,1)S(1)}, u32[]{:S(2)}, u32[]{:S(2)}) collective-permute-start(bf16[128,3072]{1,0:T(8,128)(2,1)} %bitcast.125), channel_id=1, source_target_pairs={{0,7},{1,0},{2,1},{3,2},{4,3},{5,4},{6,5},{7,6},{8,15},{9,8},{10,9... | collective-permute-start | bytes 2359304 | tf_op jit(solution)/shard_map/ppermute | solution.py:23
  44.2 35.2 %collective-permute-start.4 = (bf16[128,3072]{1,0:T(8,128)(2,1)S(1)}, bf16[128,3072]{1,0:T(8,128)(2,1)S(1)}, u32[]{:S(2)}, u32[]{:S(2)}) collective-permute-start(bf16[128,3072]{1,0:T(8,128)(2,1)S(1)} %collective-permute-done.2), channel_id=1, source_target_pairs={{0,1},{1,2},{2,3},{3,4},{4,5},{5,6},{6,7},{7,0},{8,9},{9,10},{10,1... | collective-permute-start | bytes 2359304 | tf_op jit(solution)/shard_map/ppermute | solution.py:20
  47.3 87.2 %copy-start.5 = (bf16[1,512,1024]{2,1,0:T(8,128)(2,1)S(1)}, bf16[1,512,1024]{2,1,0:T(8,128)(2,1)}, u32[]{:S(2)}) copy-start(bf16[1,512,1024]{2,1,0:T(8,128)(2,1)} %param.12) | copy-start | bytes 3145732
  47.4 35.1 %collective-permute-start.5 = (bf16[128,3072]{1,0:T(8,128)(2,1)S(1)}, bf16[128,3072]{1,0:T(8,128)(2,1)S(1)}, u32[]{:S(2)}, u32[]{:S(2)}) collective-permute-start(bf16[128,3072]{1,0:T(8,128)(2,1)S(1)} %collective-permute-done.3), channel_id=1, source_target_pairs={{0,7},{1,0},{2,1},{3,2},{4,3},{5,4},{6,5},{7,6},{8,15},{9,8},{10,9... | collective-permute-start | bytes 2359304 | tf_op jit(solution)/shard_map/ppermute | solution.py:23
  79.4 34.4 %collective-permute-start.6 = (bf16[128,3072]{1,0:T(8,128)(2,1)S(1)}, bf16[128,3072]{1,0:T(8,128)(2,1)S(1)}, u32[]{:S(2)}, u32[]{:S(2)}) collective-permute-start(bf16[128,3072]{1,0:T(8,128)(2,1)S(1)} %collective-permute-done.4), channel_id=1, source_target_pairs={{0,1},{1,2},{2,3},{3,4},{4,5},{5,6},{6,7},{7,0},{8,9},{9,10},{10,1... | collective-permute-start | bytes 2359304 | tf_op jit(solution)/shard_map/ppermute | solution.py:20
  82.5 51.9 %collective-permute-start.7 = (bf16[128,3072]{1,0:T(8,128)(2,1)S(1)}, bf16[128,3072]{1,0:T(8,128)(2,1)S(1)}, u32[]{:S(2)}, u32[]{:S(2)}) collective-permute-start(bf16[128,3072]{1,0:T(8,128)(2,1)S(1)} %collective-permute-done.5), channel_id=1, source_target_pairs={{0,7},{1,0},{2,1},{3,2},{4,3},{5,4},{6,5},{7,6},{8,15},{9,8},{10,9... | collective-permute-start | bytes 2359304 | tf_op jit(solution)/shard_map/ppermute | solution.py:23
  113.8 20.7 %collective-permute-start.8 = (bf16[128,3072]{1,0:T(8,128)(2,1)S(1)}, bf16[128,3072]{1,0:T(8,128)(2,1)S(1)}, u32[]{:S(2)}, u32[]{:S(2)}) collective-permute-start(bf16[128,3072]{1,0:T(8,128)(2,1)S(1)} %collective-permute-done.6), channel_id=1, source_target_pairs={{0,1},{1,2},{2,3},{3,4},{4,5},{5,6},{6,7},{7,0},{8,9},{9,10},{10,1... | collective-permute-start | bytes 2359304 | tf_op jit(solution)/shard_map/ppermute | solution.py:20
  138.2 1.6 copy-start.1
  152.0 6.4 %copy-start.7 = (s32[1,32]{1,0:T(1,128)S(1)}, s32[1,32]{1,0:T(1,128)}, u32[]{:S(2)}) copy-start(s32[1,32]{1,0:T(1,128)} %param.18) | copy-start | bytes 388
  152.0 210.3 %all-to-all-start = ((bf16[8,2,128,2048]{3,2,1,0:T(8,128)(2,1)}), bf16[8,2,128,2048]{3,2,1,0:T(8,128)(2,1)}, u32[]{:S(2)}, u32[]{:S(2)}) async-start(bf16[8,2,128,2048]{3,2,1,0:T(8,128)(2,1)} %broadcast_select_fusion.1), calls=%async_computation | async-start | bytes 16777216 | tf_op jit(solution)/shard_map/all_to_all | solution.py:115
  157.0 367.8 %all-gather.3.cloned.1.call-start = ((), (), s32[]{:S(2)}) async-start(), calls=%async_computation.3 | async-start | bytes 2359296 | tf_op jit(solution)/shard_map/all_gather | solution.py:129
  157.8 433.6 %reduce-scatter.2.cloned.1.call-start = ((), (), s32[]{:S(2)}) async-start(), calls=%async_computation.2 | async-start | bytes 2359296 | tf_op jit(solution)/shard_map/reduce_scatter | solution.py:131
  520.0 4.8 copy-start.6
  524.0 67.4 %copy-start.2 = (bf16[1,128,1024]{2,1,0:T(8,128)(2,1)S(1)}, bf16[1,128,1024]{2,1,0:T(8,128)(2,1)}, u32[]{:S(2)}) copy-start(bf16[1,128,1024]{2,1,0:T(8,128)(2,1)} %param.15) | copy-start | bytes 786436
  524.0 67.4 %copy-start.4 = (f32[1,128,1024]{2,1,0:T(8,128)S(1)}, f32[1,128,1024]{2,1,0:T(8,128)}, u32[]{:S(2)}) copy-start(f32[1,128,1024]{2,1,0:T(8,128)} %param.16) | copy-start | bytes 1572868
  592.6 2.0 collective-permute-start
Sparse Core Ops, SparseCore 0:
  160.0 167.0 all-gather.2
  524.1 67.2 reduce-scatter.1
